TPU v7x, 512 devices: a whole 4x4x16 slice. The times are simulated.
512 devices in a mesh: dp: 4 (over x), ctx: 16 (over z), mp: 8 (over y, core).
Axes of the slice: x: 4, y: 4, z: 16, core: 2. Of those that a mesh axis runs over, the one named last changes fastest.
Arguments:
- tokens: bfloat16 [4, 2048, 4096], P('dp', 'ctx'), may hold values from -52 to 52
- x_weight: bfloat16 [4096, 8192], P(('dp', 'ctx'), 'mp'), may hold values from -0.09375 to 0.09375
- bc_weight: bfloat16 [4096, 1024], P(('dp', 'ctx'), 'mp'), may hold values from -0.09375 to 0.09375
- dt_weight: bfloat16 [4096, 128], P(('dp', 'ctx'), 'mp'), may hold values from -0.0234375 to 0.0234375
- conv_x: float32 [5, 8192], P(None, 'mp'), may hold values from -0.5 to 0.5
- conv_bc: float32 [5, 1024], P(None, 'mp'), may hold values from -0.5 to 0.5
- dt_bias: float32 [128], P('mp'), may hold values from -4.5 to -2.5
- a_log: float32 [128], P('mp')
- d_skip: float32 [128], P('mp'), may hold values from 0.5 to 1.5
- norm_gain: float32 [8192], P('mp'), may hold values from 0.5 to 1.5
Outputs:
- mixer_out: bfloat16 [4, 2048, 8192], P('dp', 'ctx', 'mp')
- kurtosis: float32 [4096], P('mp')
All inputs are finite; a program needn't handle non-finite values.
Results may differ from a plain program's by a relative error of at most 0.015.
Values may be sent and summed in bfloat16 or wider, within the bound.
No kernel may reach another device: no remote copies, remote signals or barrier semaphores. Data moves between devices by JAX's collectives and lax.ppermute only.
A program may use at most 64 MiB of HBM per device.

v0:
```python
import jax
import jax.numpy as jnp
from jax import lax
from jax.sharding import PartitionSpec as P

ROOT = 64
HEADS = 128
G = 4
NS = 128
HIGH = lax.Precision.HIGHEST


def passed_along(value, axis, steps):
    count = lax.axis_size(axis)
    first, last = (max(0, -steps), min(count, count - steps))
    return lax.ppermute(value, axis, [(source, source + steps) for source in range(first, last)])


def entering(array, axis, combine, identity):
    length, place = (lax.axis_size(axis), lax.axis_index(axis))
    everything = jax.tree.map(
        lambda part, kind: lax.all_gather(part.astype(kind), axis),
        array,
        (jnp.bfloat16, jnp.bfloat16),
    )
    start = jax.tree.map(
        lambda part, zero: jnp.broadcast_to(jnp.asarray(zero, part.dtype), part.shape),
        array,
        identity,
    )

    def step(k, before):
        reached = k < place
        new = combine(
            before, jax.tree.map(lambda part, own: part[k].astype(own.dtype), everything, array)
        )
        return jax.tree.map(lambda a, b: jnp.where(reached, a, b), new, before)

    return lax.fori_loop(0, length, step, start)


def hadamard_signs(sign_order):
    row_index = lax.broadcasted_iota(jnp.int32, (sign_order, sign_order), 0)
    col_index = lax.broadcasted_iota(jnp.int32, (sign_order, sign_order), 1)
    common = jnp.bitwise_and(row_index, col_index)
    parity = jnp.zeros((sign_order, sign_order), jnp.int32)
    for bit_index in range(sign_order.bit_length() - 1):
        parity = parity + jnp.bitwise_and(jnp.right_shift(common, bit_index), 1)
    return 1.0 - 2.0 * jnp.bitwise_and(parity, 1).astype(jnp.float32)


def kurtosis_from(powers, row_count):
    average = powers[0] / row_count
    second = powers[1] / row_count - average * average
    fourth = (
        powers[3] / row_count
        - 4.0 * average * powers[2] / row_count
        + 6.0 * average * average * powers[1] / row_count
        - 3.0 * average * average * average * average
    )
    return fourth / (second * second + 1e-06)


def chain_states(earlier, later):
    return (earlier[0] * later[0], later[0][:, :, None, None] * earlier[1] + later[1])


def shards(
    tokens, x_weight, bc_weight, dt_weight, conv_x, conv_bc, dt_bias, a_log, d_skip, norm_gain
):
    tok_rows = tokens.shape[1]
    model_width = tokens.shape[2]
    signs = hadamard_signs(ROOT)
    blocks = tokens.reshape(tok_rows, ROOT, ROOT)
    first_pass = jnp.einsum(
        "tab,ac->tcb", blocks, signs.astype(jnp.bfloat16), preferred_element_type=jnp.float32
    )
    second = jnp.einsum("tcb,bd->tcd", first_pass, signs, precision=HIGH)
    rotated = (second.reshape(tok_rows, model_width) / ROOT).astype(jnp.bfloat16)
    channel_share = model_width // lax.axis_size("mp")
    own_cols = lax.dynamic_slice_in_dim(
        rotated, lax.axis_index("mp") * channel_share, channel_share, 1
    ).astype(jnp.float32)
    square = own_cols * own_cols
    powers = jnp.stack(
        [
            jnp.sum(own_cols, 0),
            jnp.sum(square, 0),
            jnp.sum(square * own_cols, 0),
            jnp.sum(square * square, 0),
        ]
    )
    row_count = float(tok_rows * lax.axis_size("dp") * lax.axis_size("ctx"))
    totals = lax.psum(powers, ("dp", "ctx"))
    kurtosis = kurtosis_from(totals, row_count)
    panels = (
        lax.all_gather(x_weight, ("dp", "ctx"), axis=0, tiled=True),
        lax.all_gather(bc_weight, ("dp", "ctx"), axis=0, tiled=True),
        lax.all_gather(dt_weight, ("dp", "ctx"), axis=0, tiled=True),
    )
    projected = tuple(
        (jnp.dot(rotated, panel, preferred_element_type=jnp.float32) for panel in panels)
    )
    x_cols = x_weight.shape[1]
    joined = jnp.concatenate(
        [projected[0].astype(jnp.bfloat16), projected[1].astype(jnp.bfloat16)], 1
    )
    dt_proj = lax.optimization_barrier(projected[2].astype(jnp.bfloat16))
    conv_taps = jnp.concatenate([conv_x, conv_bc], 1)
    kernel = conv_taps.shape[0] - 1
    rim_rows = passed_along(joined[tok_rows - (kernel - 1) :], "ctx", 1)
    padded = jnp.concatenate([rim_rows, joined], 0)
    conv_sum = conv_taps[kernel]
    for tap_index in range(kernel):
        conv_sum = conv_sum + conv_taps[tap_index] * padded[tap_index : tap_index + tok_rows]
    convolved = jax.nn.silu(conv_sum).astype(jnp.bfloat16)
    x_conv = convolved[:, :x_cols]
    group_all = lax.all_gather(convolved[:, x_cols:], "mp", axis=1, tiled=True)
    heads_dev = dt_weight.shape[1]
    head_size = x_cols // heads_dev
    per_group = HEADS // G
    groups_here = max(1, heads_dev // per_group)
    heads_local = heads_dev // groups_here
    first_group = lax.axis_index("mp") * heads_dev // per_group
    write_all = group_all[:, : G * NS].reshape(tok_rows, G, NS)
    read_all = group_all[:, G * NS :].reshape(tok_rows, G, NS)
    write_here = lax.dynamic_slice_in_dim(write_all, first_group, groups_here, 1)
    read_here = lax.dynamic_slice_in_dim(read_all, first_group, groups_here, 1)
    step_size = jax.nn.softplus(dt_proj.astype(jnp.float32) + dt_bias)
    decay_rate = step_size * jnp.exp(a_log)
    cumulative = jnp.cumsum(decay_rate, 0)
    block_end = cumulative[-1]
    causal = lax.broadcasted_iota(jnp.int32, (tok_rows, tok_rows), 0) >= lax.broadcasted_iota(
        jnp.int32, (tok_rows, tok_rows), 1
    )
    spread = cumulative.T[:, :, None] - cumulative.T[:, None, :]
    decay_mask = jnp.where(causal, jnp.exp(-jnp.where(causal, spread, 0.0)), 0.0)
    scores = jnp.einsum("tgn,sgn->gts", read_here, write_here, preferred_element_type=jnp.float32)
    weights = (
        scores[:, None]
        * decay_mask.reshape(groups_here, heads_local, tok_rows, tok_rows)
        * step_size.T.reshape(groups_here, heads_local, 1, tok_rows)
    ).astype(jnp.bfloat16)
    x_heads = x_conv.reshape(tok_rows, groups_here, heads_local, head_size)
    within_block = jnp.einsum(
        "ghts,sghp->tghp", weights, x_heads, preferred_element_type=jnp.float32
    )
    update = (
        (jnp.exp(-(block_end - cumulative)) * step_size).reshape(
            tok_rows, groups_here, heads_local
        )[..., None]
        * x_heads
    ).astype(jnp.bfloat16)
    contrib = jnp.einsum("sghp,sgn->ghpn", update, write_here, preferred_element_type=jnp.float32)
    identity = (jnp.ones((groups_here, heads_local), jnp.float32), jnp.zeros_like(contrib))
    carried = entering(
        (jnp.exp(-block_end).reshape(groups_here, heads_local), contrib),
        "ctx",
        chain_states,
        identity,
    )
    from_before = jnp.exp(-cumulative).reshape(tok_rows, groups_here, heads_local)[
        ..., None
    ] * jnp.einsum("tgn,ghpn->tghp", read_here.astype(jnp.float32), carried[1], precision=HIGH)
    output_raw = (
        within_block
        + from_before
        + d_skip.reshape(groups_here, heads_local)[None, :, :, None] * x_heads.astype(jnp.float32)
    )
    mean_square = jnp.mean(output_raw * output_raw, -1, keepdims=True)
    normed = (
        output_raw
        * lax.rsqrt(mean_square + 1e-05)
        * norm_gain.reshape(groups_here, heads_local, head_size)
    )
    return (normed.reshape(1, tok_rows, x_cols).astype(jnp.bfloat16), kurtosis)


def solution(mesh):
    return jax.shard_map(
        shards,
        mesh=mesh,
        in_specs=(
            P("dp", "ctx", None),
            P(("dp", "ctx"), "mp"),
            P(("dp", "ctx"), "mp"),
            P(("dp", "ctx"), "mp"),
            P(None, "mp"),
            P(None, "mp"),
            P("mp"),
            P("mp"),
            P("mp"),
            P("mp"),
        ),
        out_specs=(P("dp", "ctx", "mp"), P("mp")),
        check_vma=False,
    )
```

profile of v0, /device:TPU:8, one launch (start us, length us, event | category | flops | bytes accessed | tf_op | source)
XLA Modules:
  0.0 532.6 jit_solution(13258673937758941600)
XLA Ops:
  8.7 1.6 copy.40
  10.3 88.7 %all-gather.2 = bf16[64,64,16]{1,2,0:T(8,128)(2,1)S(1)} all-gather(bf16[1,64,16]{1,2,0:T(8,128)(2,1)S(1)} %bitcast.105), channel_id=1, replica_groups=mesh['dp'=4,'ctx'=16,'mp'=8] {'dp','ctx'}, dimensions={0}, use_global_device_ids=true | all-gather | bytes 133120 | tf_op jit(solution)/shard_map/all_gather | solution.py:99
  100.4 3.3 multiply_convert_fusion
  104.5 49.7 %all-gather.10.cloned.1.call-done = bf16[4096,128]{1,0:T(8,128)(2,1)} async-done(((bf16[64,128]{1,0:T(8,128)(2,1)}), bf16[4096,128]{1,0:T(8,128)(2,1)}) %all-gather.10.cloned.1.call-update) | async-done | bytes 1048592 | tf_op jit(solution)/shard_map/all_gather | solution.py:98
  154.2 1.7 convolution_convert_fusion.2
  155.9 154.7 %all-gather.8.cloned.1.call-done = bf16[4096,1024]{1,0:T(8,128)(2,1)} async-done(((bf16[64,1024]{1,0:T(8,128)(2,1)}), bf16[4096,1024]{1,0:T(8,128)(2,1)}) %all-gather.8.cloned.1.call-update) | async-done | bytes 8388624 | tf_op jit(solution)/shard_map/all_gather | solution.py:97
  310.6 4.7 convolution_convert_fusion.1
  315.3 3.7 collective-permute-start
  320.9 11.9 %all_gather.26 = bf16[128,1024]{1,0:T(8,128)(2,1)S(1)} all-gather(bf16[128,128]{1,0:T(8,128)(2,1)S(1)} %slice.84), channel_id=1, replica_groups=mesh['dp'=4,'ctx'=16,'mp'=8] {'mp'}, dimensions={1}, use_global_device_ids=true | all-gather | bytes 294912 | tf_op jit(solution)/shard_map/all_gather | solution.py:118
  334.3 28.7 %all-gather.3 = bf16[16,1,16]{2,1,0:T(2,128)(2,1)S(1)} all-gather(bf16[1,1,16]{2,1,0:T(2,128)(2,1)S(1)} %get-tuple-element.160), channel_id=2, replica_groups=mesh['dp'=4,'ctx'=16,'mp'=8] {'ctx'}, dimensions={0}, use_global_device_ids=true | all-gather | bytes 544 | tf_op jit(solution)/shard_map/all_gather | solution.py:22
  363.4 141.2 %psum.7 = f32[4,512]{1,0:T(4,128)S(1)} all-reduce(f32[4,512]{1,0:T(4,128)S(1)} %pad_maximum_fusion.1), channel_id=1, replica_groups=mesh['dp'=4,'ctx'=16,'mp'=8] {'dp','ctx'}, use_global_device_ids=true, to_apply=%region_8.9 | all-reduce | flops 2048 | bytes 16384 | tf_op jit(solution)/shard_map/psum | solution.py:94
  505.9 18.1 %while.14 = (s32[]{:T(128)}, f32[1,16,64,128]{3,2,1,0:T(8,128)S(1)}, s32[]{:T(128)}, bf16[16,1,16]{2,1,0:T(2,128)(2,1)S(1)}, bf16[16,1,16,64,128]{4,3,2,1,0:T(8,128)(2,1)}, /*index=5*/s32[]{:T(128)}, s32[]{:T(128)}) while((s32[]{:T(128)}, f32[1,16,64,128]{3,2,1,0:T(8,128)S(1)}, s32[]{:T(128)}, bf16[16,1,16]{2,1,0:T(2,128)(2,1)S(1)}, ...), condition=%wide.region_2.0_spmd.clone, body=%wide.region_1.0_spmd.clone.sunk | while | flops 655380 | bytes 1310985 | solution.py:39
  505.9 1.1 fusion.65
  507.1 1.1 fusion.65
  508.2 1.1 fusion.65
  509.3 1.1 fusion.65
  510.5 1.1 fusion.65
  511.6 1.1 fusion.65
  512.7 1.1 fusion.65
  513.8 1.1 fusion.65
  515.0 1.1 fusion.65
  516.1 1.1 fusion.65
  517.2 1.1 fusion.65
  519.5 1.1 fusion.65
  (89 shorter events, 15.0 us)
Async XLA Ops:
  7.2 3.2 copy-start.1
  7.2 147.1 %all-gather.10.cloned.1.call-start = ((), (), s32[]{:S(2)}) async-start(), calls=%async_computation.1 | async-start | bytes 1064960 | tf_op jit(solution)/shard_map/all_gather | solution.py:98
  7.9 302.7 %all-gather.8.cloned.1.call-start = ((), (), s32[]{:S(2)}) async-start(), calls=%async_computation | async-start | bytes 8519680 | tf_op jit(solution)/shard_map/all_gather | solution.py:97
  8.7 497.2 %all-gather.12.cloned.1.call-start = ((), (), s32[]{:S(2)}) async-start(), calls=%async_computation.2 | async-start | bytes 4456448 | tf_op jit(solution)/shard_map/all_gather | solution.py:22
  100.3 3.6 copy-start.5
  100.3 3.6 copy-start.4
  100.3 4.0 copy-start
  100.3 4.1 copy-start.3
  315.3 5.1 collective-permute-start
  320.8 13.4 %copy-start.2 = (f32[1024]{0:T(1024)S(1)}, f32[1024]{0:T(1024)}, u32[]{:S(2)}) copy-start(f32[1024]{0:T(1024)} %param.21) | copy-start | bytes 12292
  505.9 18.5 %copy-start.6 = (f32[16]{0:T(128)S(1)}, f32[16]{0:T(128)}, u32[]{:S(2)}) copy-start(f32[16]{0:T(128)} %param.20) | copy-start | bytes 196
Sparse Core Ops, SparseCore 0:
  10.9 143.2 all-gather.9
  157.2 153.3 all-gather.7
  334.2 75.3 all-gather.11
where the time goes:
time: 533 us
  blocking collectives  271 us (51%)
  waiting for transfers between devices  207 us (39%)
  other arithmetic  19.7 us (4%)
  between operations  14.1 us (3%)
  matrix products  12.9 us (2%)
    all_gather x1, waiting for transfers between devices, shards(): lax.all_gather(x_weight, ('dp', 'ctx'), axis=0, tiled=True)  155 us
    psum x1, blocking collectives, shards(): totals = lax.psum(powers, ('dp', 'ctx'))  141 us
    all_gather x1, blocking collectives, shards(): lax.all_gather(dt_weight, ('dp', 'ctx'), axis=0, tiled=True)  88.7 us
    all_gather x1, waiting for transfers between devices, shards(): lax.all_gather(bc_weight, ('dp', 'ctx'), axis=0, tiled=True)  49.7 us
    all_gather x1, blocking collectives, entering(): lax.all_gather(part.astype(kind), axis)  28.7 us
    select_n x16, other arithmetic, step(): return jax.tree.map(lambda a, b: jnp.where(reached, a, b), new, before)  17.5 us
    all_gather x1, blocking collectives, shards(): group_all = lax.all_gather(convolved[:, x_cols:], 'mp', axis=1, tiled=True)  11.9 us
  transfers between devices with their start and end apart: 4, of which 3 were waited for; matrix products, arithmetic and copies ran while one was open for 2% of the time, Pallas kernels for 0%

commit v1 on v0

--- a/solution.py
+++ b/solution.py
@@ -91,7 +91,9 @@
         ]
     )
     row_count = float(tok_rows * lax.axis_size("dp") * lax.axis_size("ctx"))
-    totals = lax.psum(powers, ("dp", "ctx"))
+    totals = powers
+    for mesh_axis in ("dp", "ctx"):
+        totals = lax.psum(totals, mesh_axis)
     kurtosis = kurtosis_from(totals, row_count)
     panels = (
         lax.all_gather(x_weight, ("dp", "ctx"), axis=0, tiled=True),

time: 533 us -> 437 us (0.82)
  the two profiles are of different devices: /device:TPU:8 before, /device:TPU:2 now
where the time goes in v1:
time: 437 us; the launch traced here: 436 us
  waiting for transfers between devices  214 us (49%)
  blocking collectives  167 us (38%)
  other arithmetic  19.7 us (5%)
  between operations  14.1 us (3%)
  matrix products  12.9 us (3%)
    all_gather x1, waiting for transfers between devices, shards(): lax.all_gather(x_weight, ('dp', 'ctx'), axis=0, tiled=True)  154 us
    all_gather x1, blocking collectives, shards(): lax.all_gather(dt_weight, ('dp', 'ctx'), axis=0, tiled=True)  88.2 us
    all_gather x1, waiting for transfers between devices, shards(): lax.all_gather(bc_weight, ('dp', 'ctx'), axis=0, tiled=True)  49.3 us
    psum x2, blocking collectives, shards(): totals = lax.psum(totals, mesh_axis)  37.9 us
    all_gather x1, blocking collectives, entering(): lax.all_gather(part.astype(kind), axis)  28.9 us
    select_n x16, other arithmetic, step(): return jax.tree.map(lambda a, b: jnp.where(reached, a, b), new, before)  17.5 us
    all_gather x1, blocking collectives, shards(): group_all = lax.all_gather(convolved[:, x_cols:], 'mp', axis=1, tiled=True)  12.2 us
  transfers between devices with their start and end apart: 4, of which 4 were waited for; matrix products, arithmetic and copies ran while one was open for 2% of the time, Pallas kernels for 0%

profile of v1, /device:TPU:2, one launch (start us, length us, event | category | flops | bytes accessed | tf_op | source)
XLA Modules:
  0.0 436.2 jit_solution(17702174703934169859)
XLA Ops:
  8.7 1.6 copy.40
  10.3 88.2 %all-gather.2 = bf16[64,64,16]{1,2,0:T(8,128)(2,1)S(1)} all-gather(bf16[1,64,16]{1,2,0:T(8,128)(2,1)S(1)} %bitcast.105), channel_id=1, replica_groups=mesh['dp'=4,'ctx'=16,'mp'=8] {'dp','ctx'}, dimensions={0}, use_global_device_ids=true | all-gather | bytes 133120 | tf_op jit(solution)/shard_map/all_gather | solution.py:101
  99.9 3.3 multiply_convert_fusion
  104.0 49.3 %all-gather.10.cloned.1.call-done = bf16[4096,128]{1,0:T(8,128)(2,1)} async-done(((bf16[64,128]{1,0:T(8,128)(2,1)}), bf16[4096,128]{1,0:T(8,128)(2,1)}) %all-gather.10.cloned.1.call-update) | async-done | bytes 1048592 | tf_op jit(solution)/shard_map/all_gather | solution.py:100
  153.3 1.7 convolution_convert_fusion.2
  155.0 154.5 %all-gather.8.cloned.1.call-done = bf16[4096,1024]{1,0:T(8,128)(2,1)} async-done(((bf16[64,1024]{1,0:T(8,128)(2,1)}), bf16[4096,1024]{1,0:T(8,128)(2,1)}) %all-gather.8.cloned.1.call-update) | async-done | bytes 8388624 | tf_op jit(solution)/shard_map/all_gather | solution.py:99
  309.5 4.7 %convolution_convert_fusion.1 = bf16[128,1024]{1,0:T(8,128)(2,1)S(1)} fusion(bf16[128,4096]{0,1:T(8,128)(2,1)S(1)} %bitcast.86, bf16[4096,1024]{1,0:T(8,128)(2,1)} %all-gather.8.cloned.1.call-done), kind=kOutput, calls=%fused_computation.13 | convolution fusion | flops 1073872896 | bytes 9699328 | tf_op jit(solution)/shard_map/dot_general | solution.py:104
  314.2 3.7 collective-permute-start
  319.7 12.2 %all_gather.26 = bf16[128,1024]{1,0:T(8,128)(2,1)S(1)} all-gather(bf16[128,128]{1,0:T(8,128)(2,1)S(1)} %slice.84), channel_id=1, replica_groups=mesh['dp'=4,'ctx'=16,'mp'=8] {'mp'}, dimensions={1}, use_global_device_ids=true | all-gather | bytes 294912 | tf_op jit(solution)/shard_map/all_gather | solution.py:120
  333.5 28.9 %all-gather.3 = bf16[16,1,16]{2,1,0:T(2,128)(2,1)S(1)} all-gather(bf16[1,1,16]{2,1,0:T(2,128)(2,1)S(1)} %get-tuple-element.160), channel_id=2, replica_groups=mesh['dp'=4,'ctx'=16,'mp'=8] {'ctx'}, dimensions={0}, use_global_device_ids=true | all-gather | bytes 544 | tf_op jit(solution)/shard_map/all_gather | solution.py:22
  362.7 9.4 %psum.14 = f32[4,512]{1,0:T(4,128)S(1)} all-reduce(f32[4,512]{1,0:T(4,128)S(1)} %pad_maximum_fusion.1), channel_id=1, replica_groups=mesh['dp'=4,'ctx'=16,'mp'=8] {'dp'}, use_global_device_ids=true, to_apply=%region_8.9 | all-reduce | flops 2048 | bytes 16384 | tf_op jit(solution)/shard_map/psum | solution.py:96
  372.1 28.5 %psum.15 = f32[4,512]{1,0:T(4,128)S(1)} all-reduce(f32[4,512]{1,0:T(4,128)S(1)} %psum.14), channel_id=1, replica_groups=mesh['dp'=4,'ctx'=16,'mp'=8] {'ctx'}, use_global_device_ids=true, to_apply=%region_9.10 | all-reduce | flops 2048 | bytes 16384 | tf_op jit(solution)/shard_map/psum | solution.py:96
  402.0 7.5 %all-gather.12.cloned.1.call-done = bf16[256,64,128]{2,1,0:T(8,128)(2,1)} async-done(((bf16[16,64,128]{2,1,0:T(8,128)(2,1)}), bf16[256,64,128]{2,1,0:T(8,128)(2,1)}) %all-gather.12.cloned.1.call-update) | async-done | bytes 4194320 | tf_op jit(solution)/shard_map/all_gather | solution.py:22
  409.5 18.1 %while.14 = (s32[]{:T(128)}, f32[1,16,64,128]{3,2,1,0:T(8,128)S(1)}, s32[]{:T(128)}, bf16[16,1,16]{2,1,0:T(2,128)(2,1)S(1)}, bf16[16,1,16,64,128]{4,3,2,1,0:T(8,128)(2,1)}, /*index=5*/s32[]{:T(128)}, s32[]{:T(128)}) while((s32[]{:T(128)}, f32[1,16,64,128]{3,2,1,0:T(8,128)S(1)}, s32[]{:T(128)}, bf16[16,1,16]{2,1,0:T(2,128)(2,1)S(1)}, ...), condition=%wide.region_2.0_spmd.clone, body=%wide.region_1.0_spmd.clone.sunk | while | flops 655380 | bytes 1310985 | solution.py:39
  409.5 1.1 fusion.65
  410.6 1.1 fusion.65
  411.8 1.1 fusion.65
  412.9 1.1 fusion.65
  414.0 1.1 fusion.65
  415.2 1.1 fusion.65
  416.3 1.1 fusion.65
  417.4 1.1 fusion.65
  418.5 1.1 fusion.65
  419.7 1.1 fusion.65
  (90 shorter events, 17.2 us)
Async XLA Ops:
  7.2 3.2 copy-start.1
  7.2 146.1 %all-gather.10.cloned.1.call-start = ((), (), s32[]{:S(2)}) async-start(), calls=%async_computation.1 | async-start | bytes 1064960 | tf_op jit(solution)/shard_map/all_gather | solution.py:100
  7.9 301.6 %all-gather.8.cloned.1.call-start = ((), (), s32[]{:S(2)}) async-start(), calls=%async_computation | async-start | bytes 8519680 | tf_op jit(solution)/shard_map/all_gather | solution.py:99
  8.7 400.8 %all-gather.12.cloned.1.call-start = ((), (), s32[]{:S(2)}) async-start(), calls=%async_computation.2 | async-start | bytes 4456448 | tf_op jit(solution)/shard_map/all_gather | solution.py:22
  99.8 3.6 copy-start.5
  99.8 3.6 copy-start.4
  99.8 4.0 copy-start
  99.8 4.1 copy-start.3
  314.2 5.0 %collective-permute-start = (bf16[3,1152]{1,0:T(4,128)(2,1)S(1)}, bf16[3,1152]{1,0:T(4,128)(2,1)S(1)}, u32[]{:S(2)}, u32[]{:S(2)}) collective-permute-start(bf16[3,1152]{1,0:T(4,128)(2,1)S(1)} %fusion.32), channel_id=1, source_target_pairs={{0,8},{8,16},{16,24},{24,32},{32,40},{40,48},{48,56},{56,64},{64,7... | collective-permute-start | bytes 20744 | tf_op jit(solution)/shard_map/ppermute | solution.py:16
  319.7 13.7 %copy-start.2 = (f32[1024]{0:T(1024)S(1)}, f32[1024]{0:T(1024)}, u32[]{:S(2)}) copy-start(f32[1024]{0:T(1024)} %param.21) | copy-start | bytes 12292
  409.5 18.5 %copy-start.6 = (f32[16]{0:T(128)S(1)}, f32[16]{0:T(128)}, u32[]{:S(2)}) copy-start(f32[16]{0:T(128)} %param.20) | copy-start | bytes 196
Sparse Core Ops, SparseCore 0:
  10.9 142.3 all-gather.9
  156.3 153.1 all-gather.7
  333.4 76.0 all-gather.11
